TPU v7x, 128 devices: a whole 4x4x4 slice. The times are simulated.
128 devices in a mesh: sta: 32 (over z, y, x_lo), tm: 4 (over x_hi, core).
Axes of the slice: x: 4 (x_hi: 2, x_lo: 2; x = x_hi * 2 + x_lo), y: 4, z: 4, core: 2. Of those that a mesh axis runs over, the one named last changes fastest.
Arguments:
- signal: bfloat16 [1024, 12288], P('sta', 'tm'), may hold values from -6 to 6
- fir: float32 [4, 32], replicated, may hold values from -1 to 1
- taps: int32 [4], replicated, may hold values from 16 to 32, as said below
- sources: int32 [2, 16], replicated, may hold values from 0 to 1023, as said below
Outputs:
- correlations: bfloat16 [2, 4, 16, 1024, 512], P(None, None, None, 'sta', 'tm')
Inputs may be any that keep to these rules, and one draw needn't show every extreme that they name: Each band has between 16 and 32 taps, and some band has exactly 32. `sources`: the source channels of one round are distinct.
All inputs are finite; a program needn't handle non-finite values.
Results may differ from a plain program's by a relative error of at most 0.0058.
Values may be sent and summed in bfloat16 or wider, within the bound.
No kernel may reach another device: no remote copies, remote signals or barrier semaphores. Data moves between devices by JAX's collectives and lax.ppermute only.
A program may use at most 128 MiB of HBM per device.

v0:
```python
import jax
import jax.numpy as jnp
from jax import lax
from jax.sharding import PartitionSpec as P

ROUNDS = 2
MAXLAG = 256


def passed_along(value, axis, steps):
    count = lax.axis_size(axis)
    first, last = (max(0, -steps), min(count, count - steps))
    return lax.ppermute(value, axis, [(source, source + steps) for source in range(first, last)])


def padded_2(block, sides, width):
    for axis, dim in sides:
        count = lax.axis_size(axis)
        forward = [(i, i + 1) for i in range(count - 1)]
        backward = [(target, source) for source, target in forward]
        low = lax.ppermute(
            lax.slice_in_dim(block, block.shape[dim] - width, None, axis=dim), axis, forward
        )
        high = lax.ppermute(lax.slice_in_dim(block, 0, width, axis=dim), axis, backward)
        block = jnp.concatenate([low, block, high], axis=dim)
    return block


def skew(values, count_rows):
    leading = values.shape[:-1]
    length = values.shape[-1]
    row_width = length + count_rows
    padded = jnp.concatenate([values, jnp.zeros(leading + (count_rows,), values.dtype)], axis=-1)
    repeated = jnp.tile(padded, (1,) * len(leading) + (count_rows,))
    return repeated[..., : count_rows * (row_width - 1)].reshape(
        leading + (count_rows, row_width - 1)
    )


def band_matrix(fir, taps, count_rows):
    tap_limit = fir.shape[1]
    active = jnp.arange(tap_limit, dtype=jnp.int32)[None, :] < taps[:, None]
    coefficients = jnp.where(active, fir, 0.0).astype(jnp.bfloat16)
    return skew(coefficients[:, ::-1], count_rows)


def filter_blocks(extended, fir, taps, length, block):
    tap_limit = fir.shape[1]
    channels = extended.shape[0]
    count = length // block
    main = extended[:, tap_limit - 1 :].reshape(channels, count, block)
    prefix = extended[:, :length].reshape(channels, count, block)[:, :, : tap_limit - 1]
    pieces = jnp.concatenate([prefix, main], axis=2)
    result = jnp.einsum(
        "cnu,btu->bcnt", pieces, band_matrix(fir, taps, block), preferred_element_type=jnp.float32
    )
    return result.reshape(result.shape[0], channels, length)


def correlate(traces, window, lag_count, time_block, lag_block):
    bands = traces.shape[0]
    count_src = traces.shape[1]
    length = traces.shape[2]
    channels = window.shape[1]
    turns = length // time_block
    groups = lag_count // lag_block
    span = time_block + lag_block - 1

    def step(turn, total):
        begin = turn * time_block
        block = lax.dynamic_slice_in_dim(traces, begin, time_block, 2)
        slab = lax.dynamic_slice_in_dim(window, begin, lag_count + time_block - 1, 2)
        parts = []
        for band in range(bands):
            skewed = skew(block[band], lag_block)
            slabs = jnp.stack(
                [slab[band, :, g * lag_block : g * lag_block + span] for g in range(groups)], axis=1
            )
            term = jnp.einsum("sqj,cgj->gqsc", skewed, slabs, preferred_element_type=jnp.float32)
            parts.append(term.reshape(lag_count, count_src, channels))
        return total + jnp.stack(parts, axis=1)

    empty = jnp.zeros((lag_count, bands, count_src, channels), jnp.float32)
    return lax.fori_loop(0, turns, step, empty)


def per_device(signal, fir, taps, sources):
    channels = signal.shape[0]
    samples = signal.shape[1]
    tap_limit = fir.shape[1]
    shards = lax.axis_size("tm")
    samples_all = samples * shards
    lag_count = 2 * MAXLAG
    norm_scale = samples_all ** (-0.5)
    fir_block = min(256, samples)
    widened = None
    left_rim = passed_along(signal[:, samples - (tap_limit - 1) :], "tm", 1)
    extended = jnp.concatenate([left_rim, signal], axis=1)
    filtered = filter_blocks(extended, fir, taps, samples, fir_block).astype(jnp.bfloat16)
    local_ids = sources - lax.axis_index("sta") * channels
    onehot = (local_ids[:, :, None] == jnp.arange(channels, dtype=jnp.int32)[None, None, :]).astype(
        jnp.bfloat16
    )
    results = []
    widened = padded_2(filtered, (("tm", 2),), MAXLAG)
    share = lag_count // shards
    lag_block = min(128, share)
    time_block = min(512, samples)
    for rnd in range(ROUNDS):
        traces = lax.psum(
            jnp.einsum(
                "sc,bct->bst", onehot[rnd], filtered, preferred_element_type=jnp.float32
            ).astype(jnp.bfloat16),
            "sta",
        )

        def lag_terms(start, count, traces=traces):
            return correlate(traces, widened, count, time_block, lag_block) * norm_scale

        summed = lax.psum_scatter(
            lag_terms(jnp.int32(0), share * lax.axis_size("tm")),
            "tm",
            scatter_dimension=0,
            tiled=True,
        ).astype(jnp.bfloat16)
        results.append(jnp.transpose(summed, (1, 2, 3, 0)))
    return jnp.stack(results, axis=0)


def solution(mesh):
    in_specs = (P("sta", "tm"), P(), P(), P())
    out_specs = P(None, None, None, "sta", "tm")
    return jax.shard_map(
        per_device, mesh=mesh, in_specs=in_specs, out_specs=out_specs, check_vma=False
    )
```

profile of v0, /device:TPU:1, one launch (start us, length us, event | category | flops | bytes accessed | tf_op | source)
XLA Modules:
  0.0 1204.5 jit_solution(2703139181319280235)
XLA Ops:
  30.9 278.6 %all-reduce.12.cloned.1.call-done = (bf16[4,16,3072]{2,1,0:T(8,128)(2,1)}, bf16[4,16,3072]{2,1,0:T(8,128)(2,1)}) async-done(((bf16[4,16,3072]{2,1,0:T(8,128)(2,1)}, bf16[4,16,3072]{2,1,0:T(8,128)(2,1)}), (bf16[4,16,3072]{2,1,0:T(8,128)(2,1)}, bf16[4,16,3072]{2,1,0:T(8,128)(2,1)})) %all-reduce.12.cloned.1.call-update) | async-done | bytes 786448 | tf_op jit(solution)/shard_map/psum | solution.py:110
  309.4 410.3 %while.28 = (s32[]{:T(128)}, f32[512,4,16,32]{0,3,2,1:T(8,128)}, bf16[4,32,3584]{2,1,0:T(8,128)(2,1)}, bf16[4,16,3072]{2,1,0:T(8,128)(2,1)}, s32[]{:T(128)}, /*i...) while((s32[]{:T(128)}, f32[512,4,16,32]{0,3,2,1:T(8,128)}, ...), condition=%wide.region_2.3_spmd.clone, body=%wide.region_1.2_spmd.clone.sunk | while | flops 1347940352 | bytes 132265400 | solution.py:84
  329.4 7.2 reshape.230
  343.2 7.2 reshape.232
  356.9 7.2 reshape.226
  379.6 7.2 reshape.228
  393.3 7.2 reshape.230
  420.9 7.2 reshape.226
  444.9 7.2 reshape.228
  486.2 7.2 reshape.226
  510.3 7.2 reshape.228
  537.9 7.2 reshape.232
  551.6 7.2 reshape.226
  575.6 7.2 reshape.228
  589.4 7.2 reshape.230
  603.2 7.2 reshape.232
  616.9 7.2 reshape.226
  682.1 7.2 reshape.226
  725.0 392.1 %while.29 = (s32[]{:T(128)}, f32[512,4,16,32]{0,3,2,1:T(8,128)}, bf16[4,32,3584]{2,1,0:T(8,128)(2,1)}, bf16[4,16,3072]{2,1,0:T(8,128)(2,1)}, s32[]{:T(128)}, /*i...) while((s32[]{:T(128)}, f32[512,4,16,32]{0,3,2,1:T(8,128)}, ...), condition=%wide.region_6.7_spmd.clone, body=%wide.region_5.6_spmd.clone.sunk | while | flops 1347940352 | bytes 132265400 | solution.py:84
  731.0 7.2 reshape.236
  758.5 7.6 reshape.240
  772.7 7.2 reshape.234
  795.5 7.2 reshape.236
  1123.5 71.9 %reduce-scatter.5.cloned.1.call-done = f32[128,4,16,32]{0,3,2,1:T(8,128)} async-done(((f32[512,4,16,32]{0,3,2,1:T(8,128)}), f32[128,4,16,32]{0,3,2,1:T(8,128)}) %reduce-scatter.5.cloned.1.call-update) | async-done | bytes 1048592 | tf_op jit(solution)/shard_map/reduce_scatter | solution.py:120
  (517 shorter events, 674.1 us)
Async XLA Ops:
  6.5 11.4 copy-start.6
  6.5 302.9 %all-reduce.12.cloned.1.call-start = ((), (), s32[]{:S(2)}) async-start(), calls=%async_computation.4 | async-start | bytes 1572864 | tf_op jit(solution)/shard_map/psum | solution.py:110
  7.4 10.6 collective-permute-start
  21.1 1101.1 %reduce-scatter.3.cloned.1.call-start = ((), (), s32[]{:S(2)}) async-start(), calls=%async_computation.2 | async-start | bytes 5242880 | tf_op jit(solution)/shard_map/reduce_scatter | solution.py:120
  21.1 4.4 collective-permute-start.1
  23.1 7.1 collective-permute-start.2
  724.9 470.5 %reduce-scatter.5.cloned.1.call-start = ((), (), s32[]{:S(2)}) async-start(), calls=%async_computation.3 | async-start | bytes 5242880 | tf_op jit(solution)/shard_map/reduce_scatter | solution.py:120
  780.9 4.4 copy-start.1
  780.9 4.4 copy-start.3
  780.9 4.4 copy-start.5
  845.1 4.4 copy-start.1
  845.1 4.4 copy-start.3
  845.1 4.4 copy-start.5
  910.6 4.4 copy-start.1
  910.6 4.4 copy-start.3
  910.6 4.4 copy-start.5
  976.2 4.4 copy-start.1
  976.2 4.4 copy-start.3
  976.2 4.4 copy-start.5
  1041.6 4.4 copy-start.1
  1041.6 4.4 copy-start.3
  1041.7 4.4 copy-start.5
  1107.0 4.4 copy-start.1
  1107.0 4.4 copy-start.3
  (19 other events, 82.1 us)
Sparse Core Ops, SparseCore 0:
  21.2 288.1 all-reduce.11
  725.0 73.4 reduce-scatter.2
  1122.3 73.1 reduce-scatter.4
where the time goes:
time: 1210 us; the launch traced here: 1200 us
  local copies, waits for them, and re-layouts  675 us (56%)
  waiting for transfers between devices  354 us (29%)
  other arithmetic  80.2 us (7%)
  matrix products  50 us (4%)
  loops' own time  21.5 us (2%)
  between operations  13.5 us (1%)
    reshape x49, local copies, waits for them, and re-layouts, skew(): repeated[..., :count_rows * (row_width - 1)]  349 us
    psum x1, waiting for transfers between devices, per_device(): lax.psum(jnp.einsum('sc,bct->bst', onehot[rnd], filtered, preferred_eleme...  279 us
    slice x49, local copies, waits for them, and re-layouts, skew(): repeated[..., :count_rows * (row_width - 1)]  82.5 us
    reshape x48, local copies, waits for them, and re-layouts, step(): return total + jnp.stack(parts, axis=1)  82.2 us
    while x120, local copies, waits for them, and re-layouts  72.3 us
    reduce_scatter x2, waiting for transfers between devices, per_device(): lax.psum_scatter(lag_terms(jnp.int32(0), share * lax.axis_size('tm')), 't...  72 us
    add x12, other arithmetic, step(): return total + jnp.stack(parts, axis=1)  64.7 us
    dot_general x48, matrix products, step(): jnp.einsum('sqj,cgj->gqsc', skewed, slabs, preferred_element_type=jnp.flo...  47.4 us
  transfers between devices with their start and end apart: 6, of which 3 were waited for; matrix products, arithmetic and copies ran while one was open for 34% of the time, Pallas kernels for 0%

commit v1 on v0

--- a/solution.py
+++ b/solution.py
@@ -107,11 +107,14 @@
     lag_block = min(128, share)
     time_block = min(512, samples)
     for rnd in range(ROUNDS):
-        traces = lax.psum(
-            jnp.einsum(
-                "sc,bct->bst", onehot[rnd], filtered, preferred_element_type=jnp.float32
-            ).astype(jnp.bfloat16),
-            "sta",
+        traces = jnp.sum(
+            lax.all_gather(
+                jnp.einsum(
+                    "sc,bct->bst", onehot[rnd], filtered, preferred_element_type=jnp.float32
+                ).astype(jnp.bfloat16),
+                "sta",
+            ),
+            axis=0,
         )
 
         def lag_terms(start, count, traces=traces):

time: 1210 us -> 1480 us (1.22)
  waiting for transfers between devices: 354 us -> 584 us
  loops' own time: 21.5 us -> 40.2 us
  other arithmetic: 80.2 us -> 97.4 us
    all_gather x0 -> x2, waiting for transfers between devices: none -> 533 us  [per_device(): lax.all_gather(jnp.einsum('sc,bct->bst', onehot[rnd], filtered, preferred...]
    psum x1 -> x0, waiting for transfers between devices: 279 us -> none  [per_device(): lax.psum(jnp.einsum('sc,bct->bst', onehot[rnd], filtered, preferred_eleme...]
    reduce_scatter x2, waiting for transfers between devices: 72 us -> 47.8 us  [per_device(): lax.psum_scatter(lag_terms(jnp.int32(0), share * lax.axis_size('tm')), 't...]
    another operation x2, loops' own time: 21.5 us -> 40.2 us  [correlate(): return lax.fori_loop(0, turns, step, empty)]
    reduce_sum x0 -> x2, other arithmetic: none -> 17.3 us  [per_device(): jnp.sum(lax.all_gather(jnp.einsum('sc,bct->bst', onehot[rnd], filtered, p...]
  transfers between devices with their start and end apart: 6 -> 7, of which waited for: 3 -> 4; matrix products, arithmetic and copies ran while one was open for 34% -> 28% of each run, Pallas kernels for 0% -> 0%
where the time goes in v1:
time: 1480 us; the launch traced here: 1470 us
  local copies, waits for them, and re-layouts  673 us (45%)
  waiting for transfers between devices  584 us (39%)
  other arithmetic  97.4 us (7%)
  matrix products  50 us (3%)
  loops' own time  40.2 us (3%)
    all_gather x2, waiting for transfers between devices, per_device(): lax.all_gather(jnp.einsum('sc,bct->bst', onehot[rnd], filtered, preferred...  533 us
    reshape x49, local copies, waits for them, and re-layouts, skew(): repeated[..., :count_rows * (row_width - 1)]  349 us
    reshape x48, local copies, waits for them, and re-layouts, step(): return total + jnp.stack(parts, axis=1)  81.8 us
    slice x49, local copies, waits for them, and re-layouts, skew(): repeated[..., :count_rows * (row_width - 1)]  80.4 us
    while x120, local copies, waits for them, and re-layouts  72.3 us
    add x12, other arithmetic, step(): return total + jnp.stack(parts, axis=1)  64.6 us
    reduce_scatter x2, waiting for transfers between devices, per_device(): lax.psum_scatter(lag_terms(jnp.int32(0), share * lax.axis_size('tm')), 't...  47.8 us
    dot_general x48, matrix products, step(): jnp.einsum('sqj,cgj->gqsc', skewed, slabs, preferred_element_type=jnp.flo...  47.4 us
  transfers between devices with their start and end apart: 7, of which 4 were waited for; matrix products, arithmetic and copies ran while one was open for 28% of the time, Pallas kernels for 0%

profile of v1, /device:TPU:1, one launch (start us, length us, event | category | flops | bytes accessed | tf_op | source)
XLA Modules:
  0.0 1468.5 jit_solution(1329392528924820154)
XLA Ops:
  31.8 265.4 %all-gather.5.cloned.1.call-done = bf16[128,16,3072]{2,1,0:T(8,128)(2,1)} async-done(((bf16[4,16,3072]{2,1,0:T(8,128)(2,1)}), bf16[128,16,3072]{2,1,0:T(8,128)(2,1)}) %all-gather.5.cloned.1.call-update) | async-done | bytes 12582928 | tf_op jit(solution)/shard_map/all_gather | solution.py:111
  297.2 8.7 reduce_sum.24
  305.8 267.2 %all-gather.7.cloned.1.call-done = bf16[128,16,3072]{2,1,0:T(8,128)(2,1)} async-done(((bf16[4,16,3072]{2,1,0:T(8,128)(2,1)}), bf16[128,16,3072]{2,1,0:T(8,128)(2,1)}) %all-gather.7.cloned.1.call-update) | async-done | bytes 12582928 | tf_op jit(solution)/shard_map/all_gather | solution.py:111
  573.0 8.7 reduce_sum.25
  581.7 408.5 %while.29 = (s32[]{:T(128)}, f32[512,4,16,32]{0,3,2,1:T(8,128)}, bf16[4,32,3584]{2,1,0:T(8,128)(2,1)}, bf16[4,16,3072]{2,1,0:T(8,128)(2,1)}, s32[]{:T(128)}, /*i...) while((s32[]{:T(128)}, f32[512,4,16,32]{0,3,2,1:T(8,128)}, ...), condition=%wide.region_6.7_spmd.clone, body=%wide.region_5.6_spmd.clone.sunk | while | flops 1347940352 | bytes 132265400 | solution.py:84
  606.5 7.2 reshape.242
  620.2 7.2 reshape.240
  647.6 7.2 reshape.236
  670.4 7.2 reshape.242
  684.1 7.2 reshape.240
  697.8 7.2 reshape.238
  711.5 7.2 reshape.236
  749.2 7.2 reshape.240
  776.7 7.2 reshape.236
  841.8 7.2 reshape.236
  865.7 7.2 reshape.242
  879.5 7.2 reshape.240
  893.2 7.2 reshape.238
  906.9 7.2 reshape.236
  930.9 7.2 reshape.242
  944.6 7.2 reshape.240
  958.3 7.2 reshape.238
  995.3 409.6 %while.28 = (s32[]{:T(128)}, f32[512,4,16,32]{0,3,2,1:T(8,128)}, bf16[4,32,3584]{2,1,0:T(8,128)(2,1)}, bf16[4,16,3072]{2,1,0:T(8,128)(2,1)}, s32[]{:T(128)}, /*i...) while((s32[]{:T(128)}, f32[512,4,16,32]{0,3,2,1:T(8,128)}, ...), condition=%wide.region_2.3_spmd.clone, body=%wide.region_1.2_spmd.clone.sunk | while | flops 1347940352 | bytes 132265400 | solution.py:84
  1411.4 47.8 %reduce-scatter.3.cloned.1.call-done = f32[128,4,16,32]{0,3,2,1:T(8,128)} async-done(((f32[512,4,16,32]{0,3,2,1:T(8,128)}), f32[128,4,16,32]{0,3,2,1:T(8,128)}) %reduce-scatter.3.cloned.1.call-update) | async-done | bytes 1048592 | tf_op jit(solution)/shard_map/reduce_scatter | solution.py:123
  (522 shorter events, 694.0 us)
Async XLA Ops:
  6.5 12.4 copy-start.6
  6.5 290.6 %all-gather.5.cloned.1.call-start = ((), (), s32[]{:S(2)}) async-start(), calls=%async_computation.4 | async-start | bytes 12976128 | tf_op jit(solution)/shard_map/all_gather | solution.py:111
  7.4 11.5 collective-permute-start
  21.0 552.0 %all-gather.7.cloned.1.call-start = ((), (), s32[]{:S(2)}) async-start(), calls=%async_computation.5 | async-start | bytes 12976128 | tf_op jit(solution)/shard_map/all_gather | solution.py:111
  22.1 1388.0 %reduce-scatter.5.cloned.1.call-start = ((), (), s32[]{:S(2)}) async-start(), calls=%async_computation.3 | async-start | bytes 5242880 | tf_op jit(solution)/shard_map/reduce_scatter | solution.py:123
  22.1 4.4 collective-permute-start.1
  24.1 7.1 collective-permute-start.2
  655.9 4.3 copy-start
  655.9 4.3 copy-start.2
  719.7 4.3 copy-start
  719.7 4.3 copy-start.2
  784.9 4.3 copy-start
  784.9 4.3 copy-start.2
  850.0 4.3 copy-start
  850.0 4.3 copy-start.2
  915.1 4.3 copy-start
  980.3 4.3 copy-start
  995.3 464.0 %reduce-scatter.3.cloned.1.call-start = ((), (), s32[]{:S(2)}) async-start(), calls=%async_computation.2 | async-start | bytes 5242880 | tf_op jit(solution)/shard_map/reduce_scatter | solution.py:123
  1070.0 4.3 copy-start.1
  1134.0 4.3 copy-start.1
  1199.3 4.3 copy-start.1
  1264.5 4.3 copy-start.1
  1329.8 4.3 copy-start.1
  1395.0 4.3 copy-start.1
  (20 other events, 86.5 us)
Sparse Core Ops, SparseCore 0:
  21.1 275.9 all-gather.4
  298.8 274.1 all-gather.6
  995.4 48.7 reduce-scatter.4
  1410.2 48.9 reduce-scatter.2
